TPU v7x, 32 devices: a whole 2x2x4 slice. The times are simulated.
32 devices in a mesh: tm: 8 (over y, x, core), space: 4 (over z).
Axes of the slice: x: 2, y: 2, z: 4, core: 2. Of those that a mesh axis runs over, the one named last changes fastest.
Arguments:
- starts: float32 [8, 32, 128, 128], P('tm', 'space'), may hold values from -6 to 6
- diffusivity: float32 [32, 128, 128], P('space'), may hold values from 0.04 to 0.2
- velocity: float32 [2, 32, 128, 128], P(None, 'space'), may hold values from -0.1 to 0.1
- obstacle: int32 [32, 128, 128], P('space'), may hold values from 0 to 1, as said below
- substep_scale: float32 [12], replicated, may hold values from 0.5 to 1
- neighbors: int32 [32, 4], P('space'), may hold values from 0 to 32, as said below
- coarse_x: float32 [32, 64, 64], P('space'), may hold values from -1 to 1
- coarse_y: float32 [32, 128, 128], P('space'), may hold values from -1 to 1
Outputs:
- slice_ends: float32 [8, 32, 128, 128], P('tm', 'space')
- increment: float32 [8, 32, 128, 128], P('tm', 'space')
Inputs may be any that keep to these rules, and one draw needn't show every extreme that they name: `neighbors`: tiles form a grid of 4 by 8; each entry names the tile beside a tile in the given direction, or 32 on the grid's edge. The tiles 8 * k to 8 * (k + 1) - 1 fill grid row k, in any order within it, so a neighbour's number differs from the tile's block k by at most one block. `obstacle`: each tile holds one tube, a disc of radius 128 // 8 to 32 cells.
All inputs are finite; a program needn't handle non-finite values.
Results may differ from a plain program's by a relative error of at most 0.0002.
Values sent between devices are 32-bit elements; how exact they have to be, the bound alone decides.
No kernel may reach another device: no remote copies, remote signals or barrier semaphores. Data moves between devices by JAX's collectives and lax.ppermute only.
A program may use at most 128 MiB of HBM per device.

v0:
```python
import jax
import jax.numpy as jnp
from jax import lax
from jax.sharding import PartitionSpec as P

SUB = 12
exact_precision = lax.Precision.HIGHEST


def padded(block, sides, width):
    for axis, dim in sides:
        count = lax.axis_size(axis)
        forward = [(i, i + 1) for i in range(count - 1)]
        backward = [(target, source) for source, target in forward]
        low = lax.ppermute(
            lax.slice_in_dim(block, block.shape[dim] - width, None, axis=dim), axis, forward
        )
        high = lax.ppermute(lax.slice_in_dim(block, 0, width, axis=dim), axis, backward)
        block = jnp.concatenate([low, block, high], axis=dim)
    return block


def spread(value, axis, source):
    kept = jnp.where(lax.axis_index(axis) == source, value, 0).astype(value.dtype)
    return lax.psum(kept, axis)


def passed_along(block, axis, distance):
    devices = range(lax.axis_size(axis))
    route = [(i - distance, i) for i in devices if i - distance in devices]
    return lax.ppermute(block, axis, route)


def restrict(values):
    return 0.5 * (values[..., 0::2, :] + values[..., 1::2, :])


def prolong(coarse_values):
    return jnp.repeat(coarse_values, 2, axis=-2)


def apply_coarse(coarse_values, matrix_x, matrix_y):
    mixed_x = jnp.einsum("tij,...tjk->...tik", matrix_x, coarse_values, precision=exact_precision)
    return jnp.einsum("...tik,tlk->...til", mixed_x, matrix_y, precision=exact_precision)


def on_device(
    starts, diffusivity, velocity, obstacle, substep_scale, neighbors, coarse_x, coarse_y
):
    slice_count = starts.shape[0]
    tile_count = starts.shape[1]
    all_tiles = tile_count * lax.axis_size("space")
    block_base = lax.axis_index("space") * tile_count
    open_cells = 1.0 - obstacle.astype(jnp.float32)
    speed_x = velocity[0]
    speed_y = velocity[1]
    shifted = neighbors - block_base + tile_count
    lookup_index = jnp.where(neighbors == all_tiles, 3 * tile_count, shifted)

    def advance(substep_index, current):
        strength = substep_scale[substep_index]
        own_faces = jnp.stack(
            [current[:, :, 0, :], current[:, :, -1, :], current[:, :, :, 0], current[:, :, :, -1]],
            axis=2,
        )
        gathered = padded(own_faces, (("space", 1),), tile_count)
        gathered = jnp.concatenate([gathered, jnp.zeros_like(gathered[:, :1])], axis=1)
        west_face = gathered[:, lookup_index[:, 0], 1]
        east_face = gathered[:, lookup_index[:, 1], 0]
        south_face = gathered[:, lookup_index[:, 2], 3]
        north_face = gathered[:, lookup_index[:, 3], 2]
        from_west = jnp.concatenate([west_face[:, :, None, :], current[:, :, :-1, :]], axis=2)
        from_east = jnp.concatenate([current[:, :, 1:, :], east_face[:, :, None, :]], axis=2)
        from_south = jnp.concatenate([south_face[:, :, :, None], current[:, :, :, :-1]], axis=3)
        from_north = jnp.concatenate([current[:, :, :, 1:], north_face[:, :, :, None]], axis=3)
        laplace = from_west + from_east + from_south + from_north - 4.0 * current
        transport = speed_x * (from_east - from_west) + speed_y * (from_north - from_south)
        return open_cells * (current + strength * diffusivity * laplace - 0.5 * transport)

    fine_ends = lax.fori_loop(0, SUB, advance, starts)
    correction = fine_ends - prolong(apply_coarse(restrict(starts), coarse_x, coarse_y))
    coarse_jump = restrict(correction)
    first_coarse = spread(restrict(starts[0]), "tm", 0)
    every_jump = lax.all_gather(coarse_jump, "tm", axis=0, tiled=True)

    def sweep(state_now, jump):
        return (apply_coarse(state_now, coarse_x, coarse_y) + jump, state_now)

    last_state, history = lax.scan(sweep, first_coarse, every_jump)
    own_coarse = lax.dynamic_slice_in_dim(
        history, lax.axis_index("tm") * slice_count, slice_count, 0
    )
    slice_ends = prolong(apply_coarse(own_coarse, coarse_x, coarse_y)) + correction
    previous = passed_along(slice_ends[-1], "tm", 1)
    first_step = jnp.where(
        lax.axis_index("tm") == 0, jnp.zeros_like(previous), previous - starts[0]
    )
    increment = jnp.concatenate([first_step[None], slice_ends[:-1] - starts[1:]], axis=0)
    return (slice_ends, increment)


def solution(mesh):
    placed = (
        P("tm", "space", None, None),
        P("space", None, None),
        P(None, "space", None, None),
        P("space", None, None),
        P(),
        P("space", None),
        P("space", None, None),
        P("space", None, None),
    )
    return jax.shard_map(
        on_device,
        mesh=mesh,
        in_specs=placed,
        out_specs=(P("tm", "space", None, None), P("tm", "space", None, None)),
        check_vma=False,
    )
```

profile of v0, /device:TPU:4, one launch (start us, length us, event | category | flops | bytes accessed | tf_op | source)
XLA Modules:
  0.0 285.6 jit_solution(6165159158150083791)
XLA Ops:
  16.3 170.8 %while.25 = (s32[]{:T(128)}, f32[1,8,128,128]{2,1,3,0:T(8,128)S(1)}, f32[8,128,128]{1,0,2:T(8,128)}, f32[12]{0:T(128)S(1)}, f32[8,128,128]{1,0,2:T(8,128)}, /*in...) while((s32[]{:T(128)}, ...), condition=%wide.region_2.3_spmd, body=%wide.region_1.2_spmd.sunk | while | flops 2710714 | bytes 10800037 | solution.py:80
  16.6 3.5 %collective-permute-start.1 = (f32[1,8,4,128]{3,2,1,0:T(4,128)S(1)}, f32[1,8,4,128]{3,2,1,0:T(4,128)S(1)}, u32[]{:S(2)}, u32[]{:S(2)}) collective-permute-start(f32[1,8,4,128]{3,2,1,0:T(4,128)S(1)} %pad_maximum_fusion.6), channel_id=1, source_target_pairs={{0,1},{1,2},{2,3},{4,5},{5,6},{6,7},{8,9},{9,10},{10,11},{12,13},{... | collective-permute-start | bytes 49160 | tf_op jit(solution)/shard_map/while/body/eval_jaxpr/ppermute | solution.py:15
  23.1 2.6 collective-permute-done
  28.7 3.0 %fusion.60 = f32[1,8,128,128]{2,1,3,0:T(8,128)S(1)} fusion(f32[1,8,128,128]{2,1,3,0:T(8,128)S(1)} %get-tuple-element.355, f32[8,128,128]{1,0,2:T(8,128)} %get-tuple-element.367, f32[1,8,128,128]{2,1,3,0:T(8,128)} %get-tuple-element.372, f32[1,8,128,128]{2,1,3,0:T(8,128)} %get-tuple-element.371, f32[1,8,128,1]{2,1,3,0:T(8,128)S(1)} %bitcast.113, ...), kind=kLoop, calls=%fused_computation.13.clone.1 | loop fusion | flops 2621440 | bytes 5242884 | tf_op jit(solution)/shard_map/while/body/eval_jaxpr/mul | solution.py:78
  31.9 3.5 %collective-permute-start.1 = (f32[1,8,4,128]{3,2,1,0:T(4,128)S(1)}, f32[1,8,4,128]{3,2,1,0:T(4,128)S(1)}, u32[]{:S(2)}, u32[]{:S(2)}) collective-permute-start(f32[1,8,4,128]{3,2,1,0:T(4,128)S(1)} %pad_maximum_fusion.6), channel_id=1, source_target_pairs={{0,1},{1,2},{2,3},{4,5},{5,6},{6,7},{8,9},{9,10},{10,11},{12,13},{... | collective-permute-start | bytes 49160 | tf_op jit(solution)/shard_map/while/body/eval_jaxpr/ppermute | solution.py:15
  38.5 2.6 collective-permute-done
  44.0 3.0 %fusion.60 = f32[1,8,128,128]{2,1,3,0:T(8,128)S(1)} fusion(f32[1,8,128,128]{2,1,3,0:T(8,128)S(1)} %get-tuple-element.355, f32[8,128,128]{1,0,2:T(8,128)} %get-tuple-element.367, f32[1,8,128,128]{2,1,3,0:T(8,128)} %get-tuple-element.372, f32[1,8,128,128]{2,1,3,0:T(8,128)} %get-tuple-element.371, f32[1,8,128,1]{2,1,3,0:T(8,128)S(1)} %bitcast.113, ...), kind=kLoop, calls=%fused_computation.13.clone.1 | loop fusion | flops 2621440 | bytes 5242884 | tf_op jit(solution)/shard_map/while/body/eval_jaxpr/mul | solution.py:78
  47.3 3.5 %collective-permute-start.1 = (f32[1,8,4,128]{3,2,1,0:T(4,128)S(1)}, f32[1,8,4,128]{3,2,1,0:T(4,128)S(1)}, u32[]{:S(2)}, u32[]{:S(2)}) collective-permute-start(f32[1,8,4,128]{3,2,1,0:T(4,128)S(1)} %pad_maximum_fusion.6), channel_id=1, source_target_pairs={{0,1},{1,2},{2,3},{4,5},{5,6},{6,7},{8,9},{9,10},{10,11},{12,13},{... | collective-permute-start | bytes 49160 | tf_op jit(solution)/shard_map/while/body/eval_jaxpr/ppermute | solution.py:15
  53.9 2.6 collective-permute-done
  59.4 3.0 %fusion.60 = f32[1,8,128,128]{2,1,3,0:T(8,128)S(1)} fusion(f32[1,8,128,128]{2,1,3,0:T(8,128)S(1)} %get-tuple-element.355, f32[8,128,128]{1,0,2:T(8,128)} %get-tuple-element.367, f32[1,8,128,128]{2,1,3,0:T(8,128)} %get-tuple-element.372, f32[1,8,128,128]{2,1,3,0:T(8,128)} %get-tuple-element.371, f32[1,8,128,1]{2,1,3,0:T(8,128)S(1)} %bitcast.113, ...), kind=kLoop, calls=%fused_computation.13.clone.1 | loop fusion | flops 2621440 | bytes 5242884 | tf_op jit(solution)/shard_map/while/body/eval_jaxpr/mul | solution.py:78
  62.7 2.0 collective-permute-start.1
  67.7 2.6 collective-permute-done
  73.3 3.0 %fusion.60 = f32[1,8,128,128]{2,1,3,0:T(8,128)S(1)} fusion(f32[1,8,128,128]{2,1,3,0:T(8,128)S(1)} %get-tuple-element.355, f32[8,128,128]{1,0,2:T(8,128)} %get-tuple-element.367, f32[1,8,128,128]{2,1,3,0:T(8,128)} %get-tuple-element.372, f32[1,8,128,128]{2,1,3,0:T(8,128)} %get-tuple-element.371, f32[1,8,128,1]{2,1,3,0:T(8,128)S(1)} %bitcast.113, ...), kind=kLoop, calls=%fused_computation.13.clone.1 | loop fusion | flops 2621440 | bytes 5242884 | tf_op jit(solution)/shard_map/while/body/eval_jaxpr/mul | solution.py:78
  76.5 2.0 collective-permute-start.1
  81.6 2.6 collective-permute-done
  87.1 3.0 %fusion.60 = f32[1,8,128,128]{2,1,3,0:T(8,128)S(1)} fusion(f32[1,8,128,128]{2,1,3,0:T(8,128)S(1)} %get-tuple-element.355, f32[8,128,128]{1,0,2:T(8,128)} %get-tuple-element.367, f32[1,8,128,128]{2,1,3,0:T(8,128)} %get-tuple-element.372, f32[1,8,128,128]{2,1,3,0:T(8,128)} %get-tuple-element.371, f32[1,8,128,1]{2,1,3,0:T(8,128)S(1)} %bitcast.113, ...), kind=kLoop, calls=%fused_computation.13.clone.1 | loop fusion | flops 2621440 | bytes 5242884 | tf_op jit(solution)/shard_map/while/body/eval_jaxpr/mul | solution.py:78
  90.4 2.0 collective-permute-start.1
  95.5 2.6 collective-permute-done
  101.0 3.0 %fusion.60 = f32[1,8,128,128]{2,1,3,0:T(8,128)S(1)} fusion(f32[1,8,128,128]{2,1,3,0:T(8,128)S(1)} %get-tuple-element.355, f32[8,128,128]{1,0,2:T(8,128)} %get-tuple-element.367, f32[1,8,128,128]{2,1,3,0:T(8,128)} %get-tuple-element.372, f32[1,8,128,128]{2,1,3,0:T(8,128)} %get-tuple-element.371, f32[1,8,128,1]{2,1,3,0:T(8,128)S(1)} %bitcast.113, ...), kind=kLoop, calls=%fused_computation.13.clone.1 | loop fusion | flops 2621440 | bytes 5242884 | tf_op jit(solution)/shard_map/while/body/eval_jaxpr/mul | solution.py:78
  104.3 2.0 collective-permute-start.1
  109.3 2.6 collective-permute-done
  114.9 3.0 %fusion.60 = f32[1,8,128,128]{2,1,3,0:T(8,128)S(1)} fusion(f32[1,8,128,128]{2,1,3,0:T(8,128)S(1)} %get-tuple-element.355, f32[8,128,128]{1,0,2:T(8,128)} %get-tuple-element.367, f32[1,8,128,128]{2,1,3,0:T(8,128)} %get-tuple-element.372, f32[1,8,128,128]{2,1,3,0:T(8,128)} %get-tuple-element.371, f32[1,8,128,1]{2,1,3,0:T(8,128)S(1)} %bitcast.113, ...), kind=kLoop, calls=%fused_computation.13.clone.1 | loop fusion | flops 2621440 | bytes 5242884 | tf_op jit(solution)/shard_map/while/body/eval_jaxpr/mul | solution.py:78
  118.1 2.0 collective-permute-start.1
  123.2 2.6 collective-permute-done
  128.7 3.0 %fusion.60 = f32[1,8,128,128]{2,1,3,0:T(8,128)S(1)} fusion(f32[1,8,128,128]{2,1,3,0:T(8,128)S(1)} %get-tuple-element.355, f32[8,128,128]{1,0,2:T(8,128)} %get-tuple-element.367, f32[1,8,128,128]{2,1,3,0:T(8,128)} %get-tuple-element.372, f32[1,8,128,128]{2,1,3,0:T(8,128)} %get-tuple-element.371, f32[1,8,128,1]{2,1,3,0:T(8,128)S(1)} %bitcast.113, ...), kind=kLoop, calls=%fused_computation.13.clone.1 | loop fusion | flops 2621440 | bytes 5242884 | tf_op jit(solution)/shard_map/while/body/eval_jaxpr/mul | solution.py:78
  132.0 2.0 collective-permute-start.1
  137.0 2.6 collective-permute-done
  142.6 3.0 %fusion.60 = f32[1,8,128,128]{2,1,3,0:T(8,128)S(1)} fusion(f32[1,8,128,128]{2,1,3,0:T(8,128)S(1)} %get-tuple-element.355, f32[8,128,128]{1,0,2:T(8,128)} %get-tuple-element.367, f32[1,8,128,128]{2,1,3,0:T(8,128)} %get-tuple-element.372, f32[1,8,128,128]{2,1,3,0:T(8,128)} %get-tuple-element.371, f32[1,8,128,1]{2,1,3,0:T(8,128)S(1)} %bitcast.113, ...), kind=kLoop, calls=%fused_computation.13.clone.1 | loop fusion | flops 2621440 | bytes 5242884 | tf_op jit(solution)/shard_map/while/body/eval_jaxpr/mul | solution.py:78
  145.8 2.0 collective-permute-start.1
  150.9 2.6 collective-permute-done
  156.4 3.0 %fusion.60 = f32[1,8,128,128]{2,1,3,0:T(8,128)S(1)} fusion(f32[1,8,128,128]{2,1,3,0:T(8,128)S(1)} %get-tuple-element.355, f32[8,128,128]{1,0,2:T(8,128)} %get-tuple-element.367, f32[1,8,128,128]{2,1,3,0:T(8,128)} %get-tuple-element.372, f32[1,8,128,128]{2,1,3,0:T(8,128)} %get-tuple-element.371, f32[1,8,128,1]{2,1,3,0:T(8,128)S(1)} %bitcast.113, ...), kind=kLoop, calls=%fused_computation.13.clone.1 | loop fusion | flops 2621440 | bytes 5242884 | tf_op jit(solution)/shard_map/while/body/eval_jaxpr/mul | solution.py:78
  159.7 2.0 collective-permute-start.1
  164.8 2.6 collective-permute-done
  170.3 3.0 %fusion.60 = f32[1,8,128,128]{2,1,3,0:T(8,128)S(1)} fusion(f32[1,8,128,128]{2,1,3,0:T(8,128)S(1)} %get-tuple-element.355, f32[8,128,128]{1,0,2:T(8,128)} %get-tuple-element.367, f32[1,8,128,128]{2,1,3,0:T(8,128)} %get-tuple-element.372, f32[1,8,128,128]{2,1,3,0:T(8,128)} %get-tuple-element.371, f32[1,8,128,1]{2,1,3,0:T(8,128)S(1)} %bitcast.113, ...), kind=kLoop, calls=%fused_computation.13.clone.1 | loop fusion | flops 2621440 | bytes 5242884 | tf_op jit(solution)/shard_map/while/body/eval_jaxpr/mul | solution.py:78
  173.6 2.0 collective-permute-start.1
  178.6 2.6 collective-permute-done
  184.2 3.0 %fusion.60 = f32[1,8,128,128]{2,1,3,0:T(8,128)S(1)} fusion(f32[1,8,128,128]{2,1,3,0:T(8,128)S(1)} %get-tuple-element.355, f32[8,128,128]{1,0,2:T(8,128)} %get-tuple-element.367, f32[1,8,128,128]{2,1,3,0:T(8,128)} %get-tuple-element.372, f32[1,8,128,128]{2,1,3,0:T(8,128)} %get-tuple-element.371, f32[1,8,128,1]{2,1,3,0:T(8,128)S(1)} %bitcast.113, ...), kind=kLoop, calls=%fused_computation.13.clone.1 | loop fusion | flops 2621440 | bytes 5242884 | tf_op jit(solution)/shard_map/while/body/eval_jaxpr/mul | solution.py:78
  187.4 1.4 convolution_bitcast_fusion.1
  191.3 26.0 %all-gather.2.cloned.1.call-done = f32[8,8,64,128]{3,2,1,0:T(8,128)} async-done(((f32[1,8,64,128]{3,2,1,0:T(8,128)}), f32[8,8,64,128]{3,2,1,0:T(8,128)}) %all-gather.2.cloned.1.call-update) | async-done | bytes 2097168 | tf_op jit(solution)/shard_map/all_gather | solution.py:84
  217.2 46.5 %while.26 = (s32[]{:T(128)}, f32[8,64,128]{2,1,0:T(8,128)}, f32[8,8,64,128]{3,2,1,0:T(8,128)}, f32[8,64,64]{2,1,0:T(8,128)S(1)}, f32[8,128,128]{2,1,0:T(8,128)S(1)}, /*index=5*/f32[8,8,64,128]{3,2,1,0:T(8,128)}, s32[]{:T(128)}) while((s32[]{:T(128)}, f32[8,64,128]{2,1,0:T(8,128)}, f32[8,8,64,128]{3,2,1,0:T(8,128)}, ...), condition=%wide.region_4.5_spmd, body=%wide.region_3.4_spmd.sunk | while | flops 151060480 | bytes 2490461 | solution.py:89
  217.2 1.3 fusion.65
  218.6 1.7 bitcast_dynamic-update-slice_fusion.2
  220.3 2.8 convolution_add_fusion.2
  223.0 1.3 fusion.65
  224.4 1.7 bitcast_dynamic-update-slice_fusion.2
  226.1 2.8 convolution_add_fusion.2
  228.9 1.3 fusion.65
  230.2 1.7 bitcast_dynamic-update-slice_fusion.2
  231.9 2.8 convolution_add_fusion.2
  234.7 1.3 fusion.65
  236.0 1.7 bitcast_dynamic-update-slice_fusion.2
  237.7 2.8 convolution_add_fusion.2
  240.5 1.3 fusion.65
  241.8 1.7 bitcast_dynamic-update-slice_fusion.2
  243.5 2.8 convolution_add_fusion.2
  247.6 1.7 bitcast_dynamic-update-slice_fusion.2
  249.3 2.8 convolution_add_fusion.2
  253.4 1.7 bitcast_dynamic-update-slice_fusion.2
  255.1 2.8 convolution_add_fusion.2
  259.2 1.7 bitcast_dynamic-update-slice_fusion.2
  260.9 2.8 convolution_add_fusion.2
  263.7 1.4 convolution_bitcast_fusion
  266.5 2.1 collective-permute-start.2
  268.6 9.3 %collective-permute-done.2 = f32[8,128,128]{2,1,0:T(8,128)S(1)} collective-permute-done((f32[8,128,128]{2,1,0:T(8,128)S(1)}, f32[8,128,128]{2,1,0:T(8,128)S(1)}, u32[]{:S(2)}, u32[]{:S(2)}) %collective-permute-start.2) | collective-permute-done | bytes 524320 | tf_op jit(solution)/shard_map/ppermute | solution.py:31
  (269 shorter events, 92.7 us)
Async XLA Ops:
  7.2 3.1 %copy-start.2 = (f32[1,8,128,128]{3,2,1,0:T(8,128)S(1)}, f32[1,8,128,128]{3,2,1,0:T(8,128)}, u32[]{:S(2)}) copy-start(f32[1,8,128,128]{3,2,1,0:T(8,128)} %param.12) | copy-start | bytes 1572868
  7.2 184.1 %all-reduce.6.cloned.1.call-start = ((), (), s32[]{:S(2)}) async-start(), calls=%async_computation | async-start | bytes 524288 | tf_op jit(solution)/shard_map/psum | solution.py:25
  7.2 4.8 %copy-start.6 = (f32[8,128,128]{2,1,0:T(8,128)S(1)}, f32[8,128,128]{2,1,0:T(8,128)}, u32[]{:S(2)}) copy-start(f32[8,128,128]{2,1,0:T(8,128)} %param.13) | copy-start | bytes 1572868
  9.4 3.6 %copy-start.7 = (s32[8,128,128]{2,1,0:T(8,128)S(1)}, s32[8,128,128]{2,1,0:T(8,128)}, u32[]{:S(2)}) copy-start(s32[8,128,128]{2,1,0:T(8,128)} %param.15) | copy-start | bytes 1572868
  10.2 207.0 %all-gather.2.cloned.1.call-start = ((), (), s32[]{:S(2)}) async-start(), calls=%async_computation.1 | async-start | bytes 2359296 | tf_op jit(solution)/shard_map/all_gather | solution.py:84
  11.8 2.3 copy-start.4
  14.1 2.1 copy-start.8
  14.1 2.1 copy-start.9
  16.3 171.1 %copy-start.1 = (f32[8,64,64]{2,1,0:T(8,128)S(1)}, f32[8,64,64]{2,1,0:T(8,128)}, u32[]{:S(2)}) copy-start(f32[8,64,64]{2,1,0:T(8,128)} %param.18) | copy-start | bytes 393220
  16.6 6.6 %collective-permute-start.1 = (f32[1,8,4,128]{3,2,1,0:T(4,128)S(1)}, f32[1,8,4,128]{3,2,1,0:T(4,128)S(1)}, u32[]{:S(2)}, u32[]{:S(2)}) collective-permute-start(f32[1,8,4,128]{3,2,1,0:T(4,128)S(1)} %pad_maximum_fusion.6), channel_id=1, source_target_pairs={{0,1},{1,2},{2,3},{4,5},{5,6},{6,7},{8,9},{9,10},{10,11},{12,13},{... | collective-permute-start | bytes 49160 | tf_op jit(solution)/shard_map/while/body/eval_jaxpr/ppermute | solution.py:15
  20.1 5.6 %collective-permute-start = (f32[1,8,4,128]{3,2,1,0:T(4,128)S(1)}, f32[1,8,4,128]{3,2,1,0:T(4,128)S(1)}, u32[]{:S(2)}, u32[]{:S(2)}) collective-permute-start(f32[1,8,4,128]{3,2,1,0:T(4,128)S(1)} %pad_maximum_fusion.6), channel_id=1, source_target_pairs={{1,0},{2,1},{3,2},{5,4},{6,5},{7,6},{9,8},{10,9},{11,10},{13,12},{... | collective-permute-start | bytes 49160 | tf_op jit(solution)/shard_map/while/body/eval_jaxpr/ppermute | solution.py:18
  31.9 6.6 %collective-permute-start.1 = (f32[1,8,4,128]{3,2,1,0:T(4,128)S(1)}, f32[1,8,4,128]{3,2,1,0:T(4,128)S(1)}, u32[]{:S(2)}, u32[]{:S(2)}) collective-permute-start(f32[1,8,4,128]{3,2,1,0:T(4,128)S(1)} %pad_maximum_fusion.6), channel_id=1, source_target_pairs={{0,1},{1,2},{2,3},{4,5},{5,6},{6,7},{8,9},{9,10},{10,11},{12,13},{... | collective-permute-start | bytes 49160 | tf_op jit(solution)/shard_map/while/body/eval_jaxpr/ppermute | solution.py:15
  35.4 5.6 %collective-permute-start = (f32[1,8,4,128]{3,2,1,0:T(4,128)S(1)}, f32[1,8,4,128]{3,2,1,0:T(4,128)S(1)}, u32[]{:S(2)}, u32[]{:S(2)}) collective-permute-start(f32[1,8,4,128]{3,2,1,0:T(4,128)S(1)} %pad_maximum_fusion.6), channel_id=1, source_target_pairs={{1,0},{2,1},{3,2},{5,4},{6,5},{7,6},{9,8},{10,9},{11,10},{13,12},{... | collective-permute-start | bytes 49160 | tf_op jit(solution)/shard_map/while/body/eval_jaxpr/ppermute | solution.py:18
  47.3 6.6 %collective-permute-start.1 = (f32[1,8,4,128]{3,2,1,0:T(4,128)S(1)}, f32[1,8,4,128]{3,2,1,0:T(4,128)S(1)}, u32[]{:S(2)}, u32[]{:S(2)}) collective-permute-start(f32[1,8,4,128]{3,2,1,0:T(4,128)S(1)} %pad_maximum_fusion.6), channel_id=1, source_target_pairs={{0,1},{1,2},{2,3},{4,5},{5,6},{6,7},{8,9},{9,10},{10,11},{12,13},{... | collective-permute-start | bytes 49160 | tf_op jit(solution)/shard_map/while/body/eval_jaxpr/ppermute | solution.py:15
  50.8 5.6 %collective-permute-start = (f32[1,8,4,128]{3,2,1,0:T(4,128)S(1)}, f32[1,8,4,128]{3,2,1,0:T(4,128)S(1)}, u32[]{:S(2)}, u32[]{:S(2)}) collective-permute-start(f32[1,8,4,128]{3,2,1,0:T(4,128)S(1)} %pad_maximum_fusion.6), channel_id=1, source_target_pairs={{1,0},{2,1},{3,2},{5,4},{6,5},{7,6},{9,8},{10,9},{11,10},{13,12},{... | collective-permute-start | bytes 49160 | tf_op jit(solution)/shard_map/while/body/eval_jaxpr/ppermute | solution.py:18
  62.7 5.1 %collective-permute-start.1 = (f32[1,8,4,128]{3,2,1,0:T(4,128)S(1)}, f32[1,8,4,128]{3,2,1,0:T(4,128)S(1)}, u32[]{:S(2)}, u32[]{:S(2)}) collective-permute-start(f32[1,8,4,128]{3,2,1,0:T(4,128)S(1)} %pad_maximum_fusion.6), channel_id=1, source_target_pairs={{0,1},{1,2},{2,3},{4,5},{5,6},{6,7},{8,9},{9,10},{10,11},{12,13},{... | collective-permute-start | bytes 49160 | tf_op jit(solution)/shard_map/while/body/eval_jaxpr/ppermute | solution.py:15
  64.7 5.6 %collective-permute-start = (f32[1,8,4,128]{3,2,1,0:T(4,128)S(1)}, f32[1,8,4,128]{3,2,1,0:T(4,128)S(1)}, u32[]{:S(2)}, u32[]{:S(2)}) collective-permute-start(f32[1,8,4,128]{3,2,1,0:T(4,128)S(1)} %pad_maximum_fusion.6), channel_id=1, source_target_pairs={{1,0},{2,1},{3,2},{5,4},{6,5},{7,6},{9,8},{10,9},{11,10},{13,12},{... | collective-permute-start | bytes 49160 | tf_op jit(solution)/shard_map/while/body/eval_jaxpr/ppermute | solution.py:18
  76.5 5.1 %collective-permute-start.1 = (f32[1,8,4,128]{3,2,1,0:T(4,128)S(1)}, f32[1,8,4,128]{3,2,1,0:T(4,128)S(1)}, u32[]{:S(2)}, u32[]{:S(2)}) collective-permute-start(f32[1,8,4,128]{3,2,1,0:T(4,128)S(1)} %pad_maximum_fusion.6), channel_id=1, source_target_pairs={{0,1},{1,2},{2,3},{4,5},{5,6},{6,7},{8,9},{9,10},{10,11},{12,13},{... | collective-permute-start | bytes 49160 | tf_op jit(solution)/shard_map/while/body/eval_jaxpr/ppermute | solution.py:15
  78.5 5.6 %collective-permute-start = (f32[1,8,4,128]{3,2,1,0:T(4,128)S(1)}, f32[1,8,4,128]{3,2,1,0:T(4,128)S(1)}, u32[]{:S(2)}, u32[]{:S(2)}) collective-permute-start(f32[1,8,4,128]{3,2,1,0:T(4,128)S(1)} %pad_maximum_fusion.6), channel_id=1, source_target_pairs={{1,0},{2,1},{3,2},{5,4},{6,5},{7,6},{9,8},{10,9},{11,10},{13,12},{... | collective-permute-start | bytes 49160 | tf_op jit(solution)/shard_map/while/body/eval_jaxpr/ppermute | solution.py:18
  90.4 5.1 %collective-permute-start.1 = (f32[1,8,4,128]{3,2,1,0:T(4,128)S(1)}, f32[1,8,4,128]{3,2,1,0:T(4,128)S(1)}, u32[]{:S(2)}, u32[]{:S(2)}) collective-permute-start(f32[1,8,4,128]{3,2,1,0:T(4,128)S(1)} %pad_maximum_fusion.6), channel_id=1, source_target_pairs={{0,1},{1,2},{2,3},{4,5},{5,6},{6,7},{8,9},{9,10},{10,11},{12,13},{... | collective-permute-start | bytes 49160 | tf_op jit(solution)/shard_map/while/body/eval_jaxpr/ppermute | solution.py:15
  92.4 5.6 %collective-permute-start = (f32[1,8,4,128]{3,2,1,0:T(4,128)S(1)}, f32[1,8,4,128]{3,2,1,0:T(4,128)S(1)}, u32[]{:S(2)}, u32[]{:S(2)}) collective-permute-start(f32[1,8,4,128]{3,2,1,0:T(4,128)S(1)} %pad_maximum_fusion.6), channel_id=1, source_target_pairs={{1,0},{2,1},{3,2},{5,4},{6,5},{7,6},{9,8},{10,9},{11,10},{13,12},{... | collective-permute-start | bytes 49160 | tf_op jit(solution)/shard_map/while/body/eval_jaxpr/ppermute | solution.py:18
  104.3 5.1 %collective-permute-start.1 = (f32[1,8,4,128]{3,2,1,0:T(4,128)S(1)}, f32[1,8,4,128]{3,2,1,0:T(4,128)S(1)}, u32[]{:S(2)}, u32[]{:S(2)}) collective-permute-start(f32[1,8,4,128]{3,2,1,0:T(4,128)S(1)} %pad_maximum_fusion.6), channel_id=1, source_target_pairs={{0,1},{1,2},{2,3},{4,5},{5,6},{6,7},{8,9},{9,10},{10,11},{12,13},{... | collective-permute-start | bytes 49160 | tf_op jit(solution)/shard_map/while/body/eval_jaxpr/ppermute | solution.py:15
  106.3 5.6 %collective-permute-start = (f32[1,8,4,128]{3,2,1,0:T(4,128)S(1)}, f32[1,8,4,128]{3,2,1,0:T(4,128)S(1)}, u32[]{:S(2)}, u32[]{:S(2)}) collective-permute-start(f32[1,8,4,128]{3,2,1,0:T(4,128)S(1)} %pad_maximum_fusion.6), channel_id=1, source_target_pairs={{1,0},{2,1},{3,2},{5,4},{6,5},{7,6},{9,8},{10,9},{11,10},{13,12},{... | collective-permute-start | bytes 49160 | tf_op jit(solution)/shard_map/while/body/eval_jaxpr/ppermute | solution.py:18
  118.1 5.1 %collective-permute-start.1 = (f32[1,8,4,128]{3,2,1,0:T(4,128)S(1)}, f32[1,8,4,128]{3,2,1,0:T(4,128)S(1)}, u32[]{:S(2)}, u32[]{:S(2)}) collective-permute-start(f32[1,8,4,128]{3,2,1,0:T(4,128)S(1)} %pad_maximum_fusion.6), channel_id=1, source_target_pairs={{0,1},{1,2},{2,3},{4,5},{5,6},{6,7},{8,9},{9,10},{10,11},{12,13},{... | collective-permute-start | bytes 49160 | tf_op jit(solution)/shard_map/while/body/eval_jaxpr/ppermute | solution.py:15
  120.1 5.6 %collective-permute-start = (f32[1,8,4,128]{3,2,1,0:T(4,128)S(1)}, f32[1,8,4,128]{3,2,1,0:T(4,128)S(1)}, u32[]{:S(2)}, u32[]{:S(2)}) collective-permute-start(f32[1,8,4,128]{3,2,1,0:T(4,128)S(1)} %pad_maximum_fusion.6), channel_id=1, source_target_pairs={{1,0},{2,1},{3,2},{5,4},{6,5},{7,6},{9,8},{10,9},{11,10},{13,12},{... | collective-permute-start | bytes 49160 | tf_op jit(solution)/shard_map/while/body/eval_jaxpr/ppermute | solution.py:18
  132.0 5.1 %collective-permute-start.1 = (f32[1,8,4,128]{3,2,1,0:T(4,128)S(1)}, f32[1,8,4,128]{3,2,1,0:T(4,128)S(1)}, u32[]{:S(2)}, u32[]{:S(2)}) collective-permute-start(f32[1,8,4,128]{3,2,1,0:T(4,128)S(1)} %pad_maximum_fusion.6), channel_id=1, source_target_pairs={{0,1},{1,2},{2,3},{4,5},{5,6},{6,7},{8,9},{9,10},{10,11},{12,13},{... | collective-permute-start | bytes 49160 | tf_op jit(solution)/shard_map/while/body/eval_jaxpr/ppermute | solution.py:15
  134.0 5.6 %collective-permute-start = (f32[1,8,4,128]{3,2,1,0:T(4,128)S(1)}, f32[1,8,4,128]{3,2,1,0:T(4,128)S(1)}, u32[]{:S(2)}, u32[]{:S(2)}) collective-permute-start(f32[1,8,4,128]{3,2,1,0:T(4,128)S(1)} %pad_maximum_fusion.6), channel_id=1, source_target_pairs={{1,0},{2,1},{3,2},{5,4},{6,5},{7,6},{9,8},{10,9},{11,10},{13,12},{... | collective-permute-start | bytes 49160 | tf_op jit(solution)/shard_map/while/body/eval_jaxpr/ppermute | solution.py:18
  145.8 5.1 %collective-permute-start.1 = (f32[1,8,4,128]{3,2,1,0:T(4,128)S(1)}, f32[1,8,4,128]{3,2,1,0:T(4,128)S(1)}, u32[]{:S(2)}, u32[]{:S(2)}) collective-permute-start(f32[1,8,4,128]{3,2,1,0:T(4,128)S(1)} %pad_maximum_fusion.6), channel_id=1, source_target_pairs={{0,1},{1,2},{2,3},{4,5},{5,6},{6,7},{8,9},{9,10},{10,11},{12,13},{... | collective-permute-start | bytes 49160 | tf_op jit(solution)/shard_map/while/body/eval_jaxpr/ppermute | solution.py:15
  147.8 5.6 %collective-permute-start = (f32[1,8,4,128]{3,2,1,0:T(4,128)S(1)}, f32[1,8,4,128]{3,2,1,0:T(4,128)S(1)}, u32[]{:S(2)}, u32[]{:S(2)}) collective-permute-start(f32[1,8,4,128]{3,2,1,0:T(4,128)S(1)} %pad_maximum_fusion.6), channel_id=1, source_target_pairs={{1,0},{2,1},{3,2},{5,4},{6,5},{7,6},{9,8},{10,9},{11,10},{13,12},{... | collective-permute-start | bytes 49160 | tf_op jit(solution)/shard_map/while/body/eval_jaxpr/ppermute | solution.py:18
  159.7 5.1 %collective-permute-start.1 = (f32[1,8,4,128]{3,2,1,0:T(4,128)S(1)}, f32[1,8,4,128]{3,2,1,0:T(4,128)S(1)}, u32[]{:S(2)}, u32[]{:S(2)}) collective-permute-start(f32[1,8,4,128]{3,2,1,0:T(4,128)S(1)} %pad_maximum_fusion.6), channel_id=1, source_target_pairs={{0,1},{1,2},{2,3},{4,5},{5,6},{6,7},{8,9},{9,10},{10,11},{12,13},{... | collective-permute-start | bytes 49160 | tf_op jit(solution)/shard_map/while/body/eval_jaxpr/ppermute | solution.py:15
  161.7 5.6 %collective-permute-start = (f32[1,8,4,128]{3,2,1,0:T(4,128)S(1)}, f32[1,8,4,128]{3,2,1,0:T(4,128)S(1)}, u32[]{:S(2)}, u32[]{:S(2)}) collective-permute-start(f32[1,8,4,128]{3,2,1,0:T(4,128)S(1)} %pad_maximum_fusion.6), channel_id=1, source_target_pairs={{1,0},{2,1},{3,2},{5,4},{6,5},{7,6},{9,8},{10,9},{11,10},{13,12},{... | collective-permute-start | bytes 49160 | tf_op jit(solution)/shard_map/while/body/eval_jaxpr/ppermute | solution.py:18
  173.6 5.1 %collective-permute-start.1 = (f32[1,8,4,128]{3,2,1,0:T(4,128)S(1)}, f32[1,8,4,128]{3,2,1,0:T(4,128)S(1)}, u32[]{:S(2)}, u32[]{:S(2)}) collective-permute-start(f32[1,8,4,128]{3,2,1,0:T(4,128)S(1)} %pad_maximum_fusion.6), channel_id=1, source_target_pairs={{0,1},{1,2},{2,3},{4,5},{5,6},{6,7},{8,9},{9,10},{10,11},{12,13},{... | collective-permute-start | bytes 49160 | tf_op jit(solution)/shard_map/while/body/eval_jaxpr/ppermute | solution.py:15
  175.6 5.6 %collective-permute-start = (f32[1,8,4,128]{3,2,1,0:T(4,128)S(1)}, f32[1,8,4,128]{3,2,1,0:T(4,128)S(1)}, u32[]{:S(2)}, u32[]{:S(2)}) collective-permute-start(f32[1,8,4,128]{3,2,1,0:T(4,128)S(1)} %pad_maximum_fusion.6), channel_id=1, source_target_pairs={{1,0},{2,1},{3,2},{5,4},{6,5},{7,6},{9,8},{10,9},{11,10},{13,12},{... | collective-permute-start | bytes 49160 | tf_op jit(solution)/shard_map/while/body/eval_jaxpr/ppermute | solution.py:18
  187.1 1.7 copy-start
  263.7 14.2 %copy-start.3 = (f32[1,8,128,128]{3,2,1,0:T(8,128)S(1)}, f32[1,8,128,128]{3,2,1,0:T(8,128)}, u32[]{:S(2)}) copy-start(f32[1,8,128,128]{3,2,1,0:T(8,128)} %param.12) | copy-start | bytes 1572868
  266.5 12.3 %copy-start.5 = (f32[1,8,128,128]{3,2,1,0:T(8,128)}, f32[1,8,128,128]{3,2,1,0:T(8,128)S(1)}, u32[]{:S(2)}) copy-start(f32[1,8,128,128]{3,2,1,0:T(8,128)S(1)} %add.163) | copy-start | bytes 1572868
  266.5 11.4 %collective-permute-start.2 = (f32[8,128,128]{2,1,0:T(8,128)S(1)}, f32[8,128,128]{2,1,0:T(8,128)S(1)}, u32[]{:S(2)}, u32[]{:S(2)}) collective-permute-start(f32[8,128,128]{2,1,0:T(8,128)S(1)} %bitcast.111), channel_id=1, source_target_pairs={{0,4},{4,8},{8,12},{12,16},{16,20},{20,24},{24,28},{1,5},{5,9},{9,... | collective-permute-start | bytes 1572872 | tf_op jit(solution)/shard_map/ppermute | solution.py:31
Sparse Core Ops, SparseCore 0:
  11.0 54.4 all-reduce.5
  191.3 25.8 all-gather.1
where the time goes:
time: 288 us; the launch traced here: 286 us
  local copies, waits for them, and re-layouts  79.5 us (28%)
  waiting for transfers between devices  66.1 us (23%)
  starting transfers between devices  46.1 us (16%)
  other arithmetic  40.4 us (14%)
  matrix products  38 us (13%)
  between operations  14.3 us (5%)
    mul x12, other arithmetic, advance(): open_cells * (current + strength * diffusivity * laplace - 0.5 * transport)  35.6 us
    ppermute x12, waiting for transfers between devices, padded(): lax.ppermute(lax.slice_in_dim(block, 0, width, axis=dim), axis, backward)  30.8 us
    ppermute x12, starting transfers between devices, padded(): lax.ppermute(lax.slice_in_dim(block, block.shape[dim] - width, None, axis...  28.3 us
    all_gather x1, waiting for transfers between devices, on_device(): every_jump = lax.all_gather(coarse_jump, 'tm', axis=0, tiled=True)  26 us
    dot_general x10, matrix products, apply_coarse(): jnp.einsum('...tik,tlk->...til', mixed_x, matrix_y, precision=exact_preci...  24.6 us
    ppermute x12, starting transfers between devices, padded(): lax.ppermute(lax.slice_in_dim(block, 0, width, axis=dim), axis, backward)  15.5 us
    dot_general x10, matrix products, apply_coarse(): jnp.einsum('tij,...tjk->...tik', matrix_x, coarse_values, precision=exact...  13.5 us
    dynamic_update_slice x8, local copies, waits for them, and re-layouts, on_device(): last_state, history = lax.scan(sweep, first_coarse, every_jump)  13.4 us
  transfers between devices with their start and end apart: 27, of which 14 were waited for; matrix products, arithmetic and copies ran while one was open for 37% of the time, Pallas kernels for 0%

commit v1 on v0

--- a/solution.py
+++ b/solution.py
@@ -1,10 +1,25 @@
+import functools
 import jax
 import jax.numpy as jnp
 from jax import lax
 from jax.sharding import PartitionSpec as P
+from jax.lax import all_to_all, psum
 
 SUB = 12
 exact_precision = lax.Precision.HIGHEST
+
+
+def balance_positions(sheet, dev_axis):
+    vals = []
+    for _ in range(psum(1, dev_axis)):
+        vals.append(sheet)
+    piece_next = jnp.concatenate(
+        all_to_all(jnp.stack(vals, axis=0), split_axis=0, axis_name=dev_axis, concat_axis=0), 0
+    )
+    return piece_next
+
+
+_lead_bands = functools.partial(balance_positions, dev_axis="tm")
 
 
 def padded(block, sides, width):
@@ -81,7 +96,7 @@
     correction = fine_ends - prolong(apply_coarse(restrict(starts), coarse_x, coarse_y))
     coarse_jump = restrict(correction)
     first_coarse = spread(restrict(starts[0]), "tm", 0)
-    every_jump = lax.all_gather(coarse_jump, "tm", axis=0, tiled=True)
+    every_jump = _lead_bands(coarse_jump)
 
     def sweep(state_now, jump):
         return (apply_coarse(state_now, coarse_x, coarse_y) + jump, state_now)

time: 288 us -> 328 us (1.14)
  waiting for transfers between devices: 66.1 us -> 100 us
  starting transfers between devices: 46.1 us -> 50.9 us
    psum x1, waiting for transfers between devices: 0.02 us -> 60.2 us  [spread(): return lax.psum(kept, axis)]
    all_gather x1 -> x0, waiting for transfers between devices: 26 us -> none  [on_device(): every_jump = lax.all_gather(coarse_jump, 'tm', axis=0, tiled=True)]
    all_to_all x0 -> x1, starting transfers between devices: none -> 4.87 us  [balance_positions(): all_to_all(jnp.stack(vals, axis=0), split_axis=0, axis_name=dev_axis, con...]
  transfers between devices with their start and end apart: 27 -> 27, of which waited for: 14 -> 14; matrix products, arithmetic and copies ran while one was open for 37% -> 7% of each run, Pallas kernels for 0% -> 0%
where the time goes in v1:
time: 328 us; the launch traced here: 325 us
  waiting for transfers between devices  100 us (30%)
  local copies, waits for them, and re-layouts  82.5 us (25%)
  starting transfers between devices  50.9 us (16%)
  other arithmetic  38.6 us (12%)
  matrix products  37.9 us (12%)
  between operations  14.3 us (4%)
    psum x1, waiting for transfers between devices, spread(): return lax.psum(kept, axis)  60.2 us
    mul x12, other arithmetic, advance(): open_cells * (current + strength * diffusivity * laplace - 0.5 * transport)  34.5 us
    ppermute x12, waiting for transfers between devices, padded(): lax.ppermute(lax.slice_in_dim(block, 0, width, axis=dim), axis, backward)  30.5 us
    ppermute x12, starting transfers between devices, padded(): lax.ppermute(lax.slice_in_dim(block, block.shape[dim] - width, None, axis...  28.6 us
    dot_general x10, matrix products, apply_coarse(): jnp.einsum('...tik,tlk->...til', mixed_x, matrix_y, precision=exact_preci...  24.6 us
    ppermute x12, starting transfers between devices, padded(): lax.ppermute(lax.slice_in_dim(block, 0, width, axis=dim), axis, backward)  15.5 us
    dynamic_update_slice x8, local copies, waits for them, and re-layouts, on_device(): last_state, history = lax.scan(sweep, first_coarse, every_jump)  13.4 us
    dot_general x10, matrix products, apply_coarse(): jnp.einsum('tij,...tjk->...tik', matrix_x, coarse_values, precision=exact...  13.3 us
  transfers between devices with their start and end apart: 27, of which 14 were waited for; matrix products, arithmetic and copies ran while one was open for 7% of the time, Pallas kernels for 0%

profile of v1, /device:TPU:4, one launch (start us, length us, event | category | flops | bytes accessed | tf_op | source)
XLA Modules:
  0.0 325.5 jit_solution(14391470796715977345)
XLA Ops:
  7.2 1.8 slice.113
  9.0 1.7 slice.112
  10.7 1.4 copy.27
  16.2 170.0 %while.25 = (s32[]{:T(128)}, f32[1,8,128,128]{2,1,3,0:T(8,128)S(1)}, f32[8,128,128]{1,0,2:T(8,128)}, f32[12]{0:T(128)S(1)}, f32[8,128,128]{1,0,2:T(8,128)}, /*in...) while((s32[]{:T(128)}, ...), condition=%wide.region_2.3_spmd, body=%wide.region_1.2_spmd.sunk | while | flops 2710714 | bytes 10800037 | solution.py:95
  16.5 3.5 %collective-permute-start.1 = (f32[1,8,4,128]{3,2,1,0:T(4,128)S(1)}, f32[1,8,4,128]{3,2,1,0:T(4,128)S(1)}, u32[]{:S(2)}, u32[]{:S(2)}) collective-permute-start(f32[1,8,4,128]{3,2,1,0:T(4,128)S(1)} %pad_maximum_fusion.6), channel_id=1, source_target_pairs={{0,1},{1,2},{2,3},{4,5},{5,6},{6,7},{8,9},{9,10},{10,11},{12,13},{... | collective-permute-start | bytes 49160 | tf_op jit(solution)/shard_map/while/body/eval_jaxpr/ppermute | solution.py:30
  23.1 2.5 collective-permute-done
  28.6 2.9 fusion.60
  31.8 3.5 %collective-permute-start.1 = (f32[1,8,4,128]{3,2,1,0:T(4,128)S(1)}, f32[1,8,4,128]{3,2,1,0:T(4,128)S(1)}, u32[]{:S(2)}, u32[]{:S(2)}) collective-permute-start(f32[1,8,4,128]{3,2,1,0:T(4,128)S(1)} %pad_maximum_fusion.6), channel_id=1, source_target_pairs={{0,1},{1,2},{2,3},{4,5},{5,6},{6,7},{8,9},{9,10},{10,11},{12,13},{... | collective-permute-start | bytes 49160 | tf_op jit(solution)/shard_map/while/body/eval_jaxpr/ppermute | solution.py:30
  38.4 2.5 collective-permute-done
  43.9 2.9 fusion.60
  47.1 3.5 %collective-permute-start.1 = (f32[1,8,4,128]{3,2,1,0:T(4,128)S(1)}, f32[1,8,4,128]{3,2,1,0:T(4,128)S(1)}, u32[]{:S(2)}, u32[]{:S(2)}) collective-permute-start(f32[1,8,4,128]{3,2,1,0:T(4,128)S(1)} %pad_maximum_fusion.6), channel_id=1, source_target_pairs={{0,1},{1,2},{2,3},{4,5},{5,6},{6,7},{8,9},{9,10},{10,11},{12,13},{... | collective-permute-start | bytes 49160 | tf_op jit(solution)/shard_map/while/body/eval_jaxpr/ppermute | solution.py:30
  53.7 2.5 collective-permute-done
  59.2 2.9 fusion.60
  62.3 2.0 collective-permute-start.1
  67.5 2.5 collective-permute-done
  73.0 2.9 fusion.60
  76.1 2.0 collective-permute-start.1
  81.3 2.5 collective-permute-done
  86.8 2.9 fusion.60
  89.9 2.0 collective-permute-start.1
  95.1 2.5 collective-permute-done
  100.6 2.9 fusion.60
  103.7 2.0 collective-permute-start.1
  108.9 2.5 collective-permute-done
  114.4 2.9 fusion.60
  117.5 2.0 collective-permute-start.1
  122.7 2.5 collective-permute-done
  128.1 2.9 fusion.60
  131.3 2.0 collective-permute-start.1
  136.4 2.5 collective-permute-done
  141.9 2.9 fusion.60
  145.1 2.0 collective-permute-start.1
  150.2 2.5 collective-permute-done
  155.7 2.9 fusion.60
  158.9 2.0 collective-permute-start.1
  164.0 2.5 collective-permute-done
  169.5 2.9 fusion.60
  172.7 2.0 collective-permute-start.1
  177.8 2.5 collective-permute-done
  183.3 2.9 fusion.60
  186.5 1.4 convolution_bitcast_fusion.1
  189.6 1.6 stack.9
  191.2 4.9 %all-to-all-start = ((f32[8,1,8,64,128]{4,3,2,1,0:T(8,128)}), f32[8,1,8,64,128]{4,3,2,1,0:T(8,128)}, u32[]{:S(2)}, u32[]{:S(2)}) async-start(f32[8,1,8,64,128]{4,3,2,1,0:T(8,128)} %stack.9), calls=%async_computation | async-start | bytes 4194304 | tf_op jit(solution)/shard_map/all_to_all | solution.py:17
  197.1 60.2 %all-reduce.6.cloned.1.call-done = f32[8,64,128]{2,1,0:T(8,128)} async-done(((f32[8,64,128]{2,1,0:T(8,128)}), f32[8,64,128]{2,1,0:T(8,128)}) %all-reduce.6.cloned.1.call-update) | async-done | bytes 262160 | tf_op jit(solution)/shard_map/psum | solution.py:40
  257.2 46.4 %while.26 = (s32[]{:T(128)}, f32[8,64,128]{2,1,0:T(8,128)}, f32[8,8,64,128]{3,2,1,0:T(8,128)}, f32[8,64,64]{2,1,0:T(8,128)S(1)}, f32[8,128,128]{2,1,0:T(8,128)S(1)}, /*index=5*/f32[8,8,64,128]{3,2,1,0:T(8,128)}, s32[]{:T(128)}) while((s32[]{:T(128)}, f32[8,64,128]{2,1,0:T(8,128)}, f32[8,8,64,128]{3,2,1,0:T(8,128)}, ...), condition=%wide.region_4.5_spmd, body=%wide.region_3.4_spmd.sunk | while | flops 151060480 | bytes 2490461 | solution.py:104
  257.2 1.3 fusion.65
  258.6 1.7 bitcast_dynamic-update-slice_fusion.2
  260.3 2.8 convolution_add_fusion.2
  264.4 1.7 bitcast_dynamic-update-slice_fusion.2
  266.1 2.8 convolution_add_fusion.2
  270.2 1.7 bitcast_dynamic-update-slice_fusion.2
  271.9 2.8 convolution_add_fusion.2
  276.0 1.7 bitcast_dynamic-update-slice_fusion.2
  277.7 2.8 convolution_add_fusion.2
  281.8 1.7 bitcast_dynamic-update-slice_fusion.2
  283.5 2.8 convolution_add_fusion.2
  287.6 1.7 bitcast_dynamic-update-slice_fusion.2
  289.3 2.8 convolution_add_fusion.2
  293.4 1.7 bitcast_dynamic-update-slice_fusion.2
  295.1 2.8 convolution_add_fusion.2
  299.2 1.7 bitcast_dynamic-update-slice_fusion.2
  300.9 2.8 convolution_add_fusion.2
  306.4 1.9 collective-permute-start.2
  308.3 9.5 %collective-permute-done.2 = f32[8,128,128]{2,1,0:T(8,128)S(1)} collective-permute-done((f32[8,128,128]{2,1,0:T(8,128)S(1)}, f32[8,128,128]{2,1,0:T(8,128)S(1)}, u32[]{:S(2)}, u32[]{:S(2)}) %collective-permute-start.2) | collective-permute-done | bytes 524320 | tf_op jit(solution)/shard_map/ppermute | solution.py:46
  (267 shorter events, 95.0 us)
Async XLA Ops:
  7.2 4.9 %copy-start.5 = (f32[8,128,128]{2,1,0:T(8,128)S(1)}, f32[8,128,128]{2,1,0:T(8,128)}, u32[]{:S(2)}) copy-start(f32[8,128,128]{2,1,0:T(8,128)} %param.13) | copy-start | bytes 1572868
  7.2 5.9 %copy-start.6 = (s32[8,128,128]{2,1,0:T(8,128)S(1)}, s32[8,128,128]{2,1,0:T(8,128)}, u32[]{:S(2)}) copy-start(s32[8,128,128]{2,1,0:T(8,128)} %param.15) | copy-start | bytes 1572868
  10.7 3.5 %copy-start.3 = (f32[2,8,128,128]{3,2,1,0:T(8,128)S(1)}, f32[2,8,128,128]{3,2,1,0:T(8,128)}, u32[]{:S(2)}) copy-start(f32[2,8,128,128]{3,2,1,0:T(8,128)} %param.14) | copy-start | bytes 3145732
  14.1 2.1 copy-start.7
  14.1 2.1 copy-start.8
  16.2 170.2 %copy-start.1 = (f32[8,64,64]{2,1,0:T(8,128)S(1)}, f32[8,64,64]{2,1,0:T(8,128)}, u32[]{:S(2)}) copy-start(f32[8,64,64]{2,1,0:T(8,128)} %param.18) | copy-start | bytes 393220
  16.5 6.6 %collective-permute-start.1 = (f32[1,8,4,128]{3,2,1,0:T(4,128)S(1)}, f32[1,8,4,128]{3,2,1,0:T(4,128)S(1)}, u32[]{:S(2)}, u32[]{:S(2)}) collective-permute-start(f32[1,8,4,128]{3,2,1,0:T(4,128)S(1)} %pad_maximum_fusion.6), channel_id=1, source_target_pairs={{0,1},{1,2},{2,3},{4,5},{5,6},{6,7},{8,9},{9,10},{10,11},{12,13},{... | collective-permute-start | bytes 49160 | tf_op jit(solution)/shard_map/while/body/eval_jaxpr/ppermute | solution.py:30
  20.0 5.6 %collective-permute-start = (f32[1,8,4,128]{3,2,1,0:T(4,128)S(1)}, f32[1,8,4,128]{3,2,1,0:T(4,128)S(1)}, u32[]{:S(2)}, u32[]{:S(2)}) collective-permute-start(f32[1,8,4,128]{3,2,1,0:T(4,128)S(1)} %pad_maximum_fusion.6), channel_id=1, source_target_pairs={{1,0},{2,1},{3,2},{5,4},{6,5},{7,6},{9,8},{10,9},{11,10},{13,12},{... | collective-permute-start | bytes 49160 | tf_op jit(solution)/shard_map/while/body/eval_jaxpr/ppermute | solution.py:33
  31.8 6.6 %collective-permute-start.1 = (f32[1,8,4,128]{3,2,1,0:T(4,128)S(1)}, f32[1,8,4,128]{3,2,1,0:T(4,128)S(1)}, u32[]{:S(2)}, u32[]{:S(2)}) collective-permute-start(f32[1,8,4,128]{3,2,1,0:T(4,128)S(1)} %pad_maximum_fusion.6), channel_id=1, source_target_pairs={{0,1},{1,2},{2,3},{4,5},{5,6},{6,7},{8,9},{9,10},{10,11},{12,13},{... | collective-permute-start | bytes 49160 | tf_op jit(solution)/shard_map/while/body/eval_jaxpr/ppermute | solution.py:30
  35.3 5.6 %collective-permute-start = (f32[1,8,4,128]{3,2,1,0:T(4,128)S(1)}, f32[1,8,4,128]{3,2,1,0:T(4,128)S(1)}, u32[]{:S(2)}, u32[]{:S(2)}) collective-permute-start(f32[1,8,4,128]{3,2,1,0:T(4,128)S(1)} %pad_maximum_fusion.6), channel_id=1, source_target_pairs={{1,0},{2,1},{3,2},{5,4},{6,5},{7,6},{9,8},{10,9},{11,10},{13,12},{... | collective-permute-start | bytes 49160 | tf_op jit(solution)/shard_map/while/body/eval_jaxpr/ppermute | solution.py:33
  47.1 6.6 %collective-permute-start.1 = (f32[1,8,4,128]{3,2,1,0:T(4,128)S(1)}, f32[1,8,4,128]{3,2,1,0:T(4,128)S(1)}, u32[]{:S(2)}, u32[]{:S(2)}) collective-permute-start(f32[1,8,4,128]{3,2,1,0:T(4,128)S(1)} %pad_maximum_fusion.6), channel_id=1, source_target_pairs={{0,1},{1,2},{2,3},{4,5},{5,6},{6,7},{8,9},{9,10},{10,11},{12,13},{... | collective-permute-start | bytes 49160 | tf_op jit(solution)/shard_map/while/body/eval_jaxpr/ppermute | solution.py:30
  50.6 5.6 %collective-permute-start = (f32[1,8,4,128]{3,2,1,0:T(4,128)S(1)}, f32[1,8,4,128]{3,2,1,0:T(4,128)S(1)}, u32[]{:S(2)}, u32[]{:S(2)}) collective-permute-start(f32[1,8,4,128]{3,2,1,0:T(4,128)S(1)} %pad_maximum_fusion.6), channel_id=1, source_target_pairs={{1,0},{2,1},{3,2},{5,4},{6,5},{7,6},{9,8},{10,9},{11,10},{13,12},{... | collective-permute-start | bytes 49160 | tf_op jit(solution)/shard_map/while/body/eval_jaxpr/ppermute | solution.py:33
  62.3 5.1 %collective-permute-start.1 = (f32[1,8,4,128]{3,2,1,0:T(4,128)S(1)}, f32[1,8,4,128]{3,2,1,0:T(4,128)S(1)}, u32[]{:S(2)}, u32[]{:S(2)}) collective-permute-start(f32[1,8,4,128]{3,2,1,0:T(4,128)S(1)} %pad_maximum_fusion.6), channel_id=1, source_target_pairs={{0,1},{1,2},{2,3},{4,5},{5,6},{6,7},{8,9},{9,10},{10,11},{12,13},{... | collective-permute-start | bytes 49160 | tf_op jit(solution)/shard_map/while/body/eval_jaxpr/ppermute | solution.py:30
  64.4 5.6 %collective-permute-start = (f32[1,8,4,128]{3,2,1,0:T(4,128)S(1)}, f32[1,8,4,128]{3,2,1,0:T(4,128)S(1)}, u32[]{:S(2)}, u32[]{:S(2)}) collective-permute-start(f32[1,8,4,128]{3,2,1,0:T(4,128)S(1)} %pad_maximum_fusion.6), channel_id=1, source_target_pairs={{1,0},{2,1},{3,2},{5,4},{6,5},{7,6},{9,8},{10,9},{11,10},{13,12},{... | collective-permute-start | bytes 49160 | tf_op jit(solution)/shard_map/while/body/eval_jaxpr/ppermute | solution.py:33
  76.1 5.1 %collective-permute-start.1 = (f32[1,8,4,128]{3,2,1,0:T(4,128)S(1)}, f32[1,8,4,128]{3,2,1,0:T(4,128)S(1)}, u32[]{:S(2)}, u32[]{:S(2)}) collective-permute-start(f32[1,8,4,128]{3,2,1,0:T(4,128)S(1)} %pad_maximum_fusion.6), channel_id=1, source_target_pairs={{0,1},{1,2},{2,3},{4,5},{5,6},{6,7},{8,9},{9,10},{10,11},{12,13},{... | collective-permute-start | bytes 49160 | tf_op jit(solution)/shard_map/while/body/eval_jaxpr/ppermute | solution.py:30
  78.2 5.6 %collective-permute-start = (f32[1,8,4,128]{3,2,1,0:T(4,128)S(1)}, f32[1,8,4,128]{3,2,1,0:T(4,128)S(1)}, u32[]{:S(2)}, u32[]{:S(2)}) collective-permute-start(f32[1,8,4,128]{3,2,1,0:T(4,128)S(1)} %pad_maximum_fusion.6), channel_id=1, source_target_pairs={{1,0},{2,1},{3,2},{5,4},{6,5},{7,6},{9,8},{10,9},{11,10},{13,12},{... | collective-permute-start | bytes 49160 | tf_op jit(solution)/shard_map/while/body/eval_jaxpr/ppermute | solution.py:33
  89.9 5.1 %collective-permute-start.1 = (f32[1,8,4,128]{3,2,1,0:T(4,128)S(1)}, f32[1,8,4,128]{3,2,1,0:T(4,128)S(1)}, u32[]{:S(2)}, u32[]{:S(2)}) collective-permute-start(f32[1,8,4,128]{3,2,1,0:T(4,128)S(1)} %pad_maximum_fusion.6), channel_id=1, source_target_pairs={{0,1},{1,2},{2,3},{4,5},{5,6},{6,7},{8,9},{9,10},{10,11},{12,13},{... | collective-permute-start | bytes 49160 | tf_op jit(solution)/shard_map/while/body/eval_jaxpr/ppermute | solution.py:30
  92.0 5.6 %collective-permute-start = (f32[1,8,4,128]{3,2,1,0:T(4,128)S(1)}, f32[1,8,4,128]{3,2,1,0:T(4,128)S(1)}, u32[]{:S(2)}, u32[]{:S(2)}) collective-permute-start(f32[1,8,4,128]{3,2,1,0:T(4,128)S(1)} %pad_maximum_fusion.6), channel_id=1, source_target_pairs={{1,0},{2,1},{3,2},{5,4},{6,5},{7,6},{9,8},{10,9},{11,10},{13,12},{... | collective-permute-start | bytes 49160 | tf_op jit(solution)/shard_map/while/body/eval_jaxpr/ppermute | solution.py:33
  103.7 5.1 %collective-permute-start.1 = (f32[1,8,4,128]{3,2,1,0:T(4,128)S(1)}, f32[1,8,4,128]{3,2,1,0:T(4,128)S(1)}, u32[]{:S(2)}, u32[]{:S(2)}) collective-permute-start(f32[1,8,4,128]{3,2,1,0:T(4,128)S(1)} %pad_maximum_fusion.6), channel_id=1, source_target_pairs={{0,1},{1,2},{2,3},{4,5},{5,6},{6,7},{8,9},{9,10},{10,11},{12,13},{... | collective-permute-start | bytes 49160 | tf_op jit(solution)/shard_map/while/body/eval_jaxpr/ppermute | solution.py:30
  105.8 5.6 %collective-permute-start = (f32[1,8,4,128]{3,2,1,0:T(4,128)S(1)}, f32[1,8,4,128]{3,2,1,0:T(4,128)S(1)}, u32[]{:S(2)}, u32[]{:S(2)}) collective-permute-start(f32[1,8,4,128]{3,2,1,0:T(4,128)S(1)} %pad_maximum_fusion.6), channel_id=1, source_target_pairs={{1,0},{2,1},{3,2},{5,4},{6,5},{7,6},{9,8},{10,9},{11,10},{13,12},{... | collective-permute-start | bytes 49160 | tf_op jit(solution)/shard_map/while/body/eval_jaxpr/ppermute | solution.py:33
  117.5 5.1 %collective-permute-start.1 = (f32[1,8,4,128]{3,2,1,0:T(4,128)S(1)}, f32[1,8,4,128]{3,2,1,0:T(4,128)S(1)}, u32[]{:S(2)}, u32[]{:S(2)}) collective-permute-start(f32[1,8,4,128]{3,2,1,0:T(4,128)S(1)} %pad_maximum_fusion.6), channel_id=1, source_target_pairs={{0,1},{1,2},{2,3},{4,5},{5,6},{6,7},{8,9},{9,10},{10,11},{12,13},{... | collective-permute-start | bytes 49160 | tf_op jit(solution)/shard_map/while/body/eval_jaxpr/ppermute | solution.py:30
  119.6 5.6 %collective-permute-start = (f32[1,8,4,128]{3,2,1,0:T(4,128)S(1)}, f32[1,8,4,128]{3,2,1,0:T(4,128)S(1)}, u32[]{:S(2)}, u32[]{:S(2)}) collective-permute-start(f32[1,8,4,128]{3,2,1,0:T(4,128)S(1)} %pad_maximum_fusion.6), channel_id=1, source_target_pairs={{1,0},{2,1},{3,2},{5,4},{6,5},{7,6},{9,8},{10,9},{11,10},{13,12},{... | collective-permute-start | bytes 49160 | tf_op jit(solution)/shard_map/while/body/eval_jaxpr/ppermute | solution.py:33
  131.3 5.1 %collective-permute-start.1 = (f32[1,8,4,128]{3,2,1,0:T(4,128)S(1)}, f32[1,8,4,128]{3,2,1,0:T(4,128)S(1)}, u32[]{:S(2)}, u32[]{:S(2)}) collective-permute-start(f32[1,8,4,128]{3,2,1,0:T(4,128)S(1)} %pad_maximum_fusion.6), channel_id=1, source_target_pairs={{0,1},{1,2},{2,3},{4,5},{5,6},{6,7},{8,9},{9,10},{10,11},{12,13},{... | collective-permute-start | bytes 49160 | tf_op jit(solution)/shard_map/while/body/eval_jaxpr/ppermute | solution.py:30
  133.4 5.6 %collective-permute-start = (f32[1,8,4,128]{3,2,1,0:T(4,128)S(1)}, f32[1,8,4,128]{3,2,1,0:T(4,128)S(1)}, u32[]{:S(2)}, u32[]{:S(2)}) collective-permute-start(f32[1,8,4,128]{3,2,1,0:T(4,128)S(1)} %pad_maximum_fusion.6), channel_id=1, source_target_pairs={{1,0},{2,1},{3,2},{5,4},{6,5},{7,6},{9,8},{10,9},{11,10},{13,12},{... | collective-permute-start | bytes 49160 | tf_op jit(solution)/shard_map/while/body/eval_jaxpr/ppermute | solution.py:33
  145.1 5.1 %collective-permute-start.1 = (f32[1,8,4,128]{3,2,1,0:T(4,128)S(1)}, f32[1,8,4,128]{3,2,1,0:T(4,128)S(1)}, u32[]{:S(2)}, u32[]{:S(2)}) collective-permute-start(f32[1,8,4,128]{3,2,1,0:T(4,128)S(1)} %pad_maximum_fusion.6), channel_id=1, source_target_pairs={{0,1},{1,2},{2,3},{4,5},{5,6},{6,7},{8,9},{9,10},{10,11},{12,13},{... | collective-permute-start | bytes 49160 | tf_op jit(solution)/shard_map/while/body/eval_jaxpr/ppermute | solution.py:30
  147.2 5.6 %collective-permute-start = (f32[1,8,4,128]{3,2,1,0:T(4,128)S(1)}, f32[1,8,4,128]{3,2,1,0:T(4,128)S(1)}, u32[]{:S(2)}, u32[]{:S(2)}) collective-permute-start(f32[1,8,4,128]{3,2,1,0:T(4,128)S(1)} %pad_maximum_fusion.6), channel_id=1, source_target_pairs={{1,0},{2,1},{3,2},{5,4},{6,5},{7,6},{9,8},{10,9},{11,10},{13,12},{... | collective-permute-start | bytes 49160 | tf_op jit(solution)/shard_map/while/body/eval_jaxpr/ppermute | solution.py:33
  158.9 5.1 %collective-permute-start.1 = (f32[1,8,4,128]{3,2,1,0:T(4,128)S(1)}, f32[1,8,4,128]{3,2,1,0:T(4,128)S(1)}, u32[]{:S(2)}, u32[]{:S(2)}) collective-permute-start(f32[1,8,4,128]{3,2,1,0:T(4,128)S(1)} %pad_maximum_fusion.6), channel_id=1, source_target_pairs={{0,1},{1,2},{2,3},{4,5},{5,6},{6,7},{8,9},{9,10},{10,11},{12,13},{... | collective-permute-start | bytes 49160 | tf_op jit(solution)/shard_map/while/body/eval_jaxpr/ppermute | solution.py:30
  160.9 5.6 %collective-permute-start = (f32[1,8,4,128]{3,2,1,0:T(4,128)S(1)}, f32[1,8,4,128]{3,2,1,0:T(4,128)S(1)}, u32[]{:S(2)}, u32[]{:S(2)}) collective-permute-start(f32[1,8,4,128]{3,2,1,0:T(4,128)S(1)} %pad_maximum_fusion.6), channel_id=1, source_target_pairs={{1,0},{2,1},{3,2},{5,4},{6,5},{7,6},{9,8},{10,9},{11,10},{13,12},{... | collective-permute-start | bytes 49160 | tf_op jit(solution)/shard_map/while/body/eval_jaxpr/ppermute | solution.py:33
  172.7 5.1 %collective-permute-start.1 = (f32[1,8,4,128]{3,2,1,0:T(4,128)S(1)}, f32[1,8,4,128]{3,2,1,0:T(4,128)S(1)}, u32[]{:S(2)}, u32[]{:S(2)}) collective-permute-start(f32[1,8,4,128]{3,2,1,0:T(4,128)S(1)} %pad_maximum_fusion.6), channel_id=1, source_target_pairs={{0,1},{1,2},{2,3},{4,5},{5,6},{6,7},{8,9},{9,10},{10,11},{12,13},{... | collective-permute-start | bytes 49160 | tf_op jit(solution)/shard_map/while/body/eval_jaxpr/ppermute | solution.py:30
  174.7 5.6 %collective-permute-start = (f32[1,8,4,128]{3,2,1,0:T(4,128)S(1)}, f32[1,8,4,128]{3,2,1,0:T(4,128)S(1)}, u32[]{:S(2)}, u32[]{:S(2)}) collective-permute-start(f32[1,8,4,128]{3,2,1,0:T(4,128)S(1)} %pad_maximum_fusion.6), channel_id=1, source_target_pairs={{1,0},{2,1},{3,2},{5,4},{6,5},{7,6},{9,8},{10,9},{11,10},{13,12},{... | collective-permute-start | bytes 49160 | tf_op jit(solution)/shard_map/while/body/eval_jaxpr/ppermute | solution.py:33
  186.2 1.7 copy-start
  191.2 4.9 %copy-start.2 = (f32[1,8,128,128]{3,2,1,0:T(8,128)S(1)}, f32[1,8,128,128]{3,2,1,0:T(8,128)}, u32[]{:S(2)}) copy-start(f32[1,8,128,128]{3,2,1,0:T(8,128)} %param.12) | copy-start | bytes 1572868
  191.2 66.1 %all-to-all-start = ((f32[8,1,8,64,128]{4,3,2,1,0:T(8,128)}), f32[8,1,8,64,128]{4,3,2,1,0:T(8,128)}, u32[]{:S(2)}, u32[]{:S(2)}) async-start(f32[8,1,8,64,128]{4,3,2,1,0:T(8,128)} %stack.9), calls=%async_computation | async-start | bytes 4194304 | tf_op jit(solution)/shard_map/all_to_all | solution.py:17
  196.1 61.2 %all-reduce.6.cloned.1.call-start = ((), (), s32[]{:S(2)}) async-start(), calls=%async_computation.1 | async-start | bytes 524288 | tf_op jit(solution)/shard_map/psum | solution.py:40
  306.4 12.3 %copy-start.4 = (f32[1,8,128,128]{3,2,1,0:T(8,128)}, f32[1,8,128,128]{3,2,1,0:T(8,128)S(1)}, u32[]{:S(2)}) copy-start(f32[1,8,128,128]{3,2,1,0:T(8,128)S(1)} %add.163) | copy-start | bytes 1572868
  306.4 11.4 %collective-permute-start.2 = (f32[8,128,128]{2,1,0:T(8,128)S(1)}, f32[8,128,128]{2,1,0:T(8,128)S(1)}, u32[]{:S(2)}, u32[]{:S(2)}) collective-permute-start(f32[8,128,128]{2,1,0:T(8,128)S(1)} %bitcast.114), channel_id=1, source_target_pairs={{0,4},{4,8},{8,12},{12,16},{16,20},{20,24},{24,28},{1,5},{5,9},{9,... | collective-permute-start | bytes 1572872 | tf_op jit(solution)/shard_map/ppermute | solution.py:46
Sparse Core Ops, SparseCore 0:
  200.5 56.7 all-reduce.5
